TPU v7x, 256 devices: a whole 4x4x8 slice. The times are simulated.
256 devices in a mesh: tensor: 2 (over core), row: 16 (over x, y), col: 8 (over z).
Axes of the slice: x: 4, y: 4, z: 8, core: 2. Of those that a mesh axis runs over, the one named last changes fastest.
Arguments:
- integral_tiles: bfloat16 [8192, 8, 4096], P(('tensor', 'row', 'col')), may hold values from -6 to 6
- tile_index: int32 [8192, 3], P(('tensor', 'row', 'col')), may hold values from 0 to 127, as said below
- virtual_coeff: bfloat16 [8192, 2048], P('col'), may hold values from -0.09375 to 0.09375
- occupied_coeff: bfloat16 [2048, 512], P('row'), may hold values from -0.125 to 0.125
Outputs:
- pair_tensor: bfloat16 [2048, 32, 512], P(('row', 'col'), 'tensor')
Inputs may be any that keep to these rules, and one draw needn't show every extreme that they name: `tile_index`: the tiles of the device at index (t, r, c) of tensor, row, col all have their nu block in c * 16 .. (c + 1) * 16 - 1, their auxiliary block below 4 and their mu block below 32. A tile's owner is (tensor index a // 2, row index m // 2) in the same col. Each device holds at most 2 tiles for any one owner; in every draw some owner gets exactly 2 tiles from every device of its col. Tiles with equal indices may occur and add up.
All inputs are finite; a program needn't handle non-finite values.
Results may differ from a plain program's by a relative error of at most 0.025.
Values may be sent and summed in bfloat16 or wider, within the bound.
No kernel may reach another device: no remote copies, remote signals or barrier semaphores. Data moves between devices by JAX's collectives and lax.ppermute only.
A program may use at most 128 MiB of HBM per device.

v0:
```python
import jax
import jax.numpy as jnp
from jax import lax
from jax.sharding import PartitionSpec as P

TB = 64
PB = 8
AB = 2
MB = 2
NBC = 16
CAP = 2
NV = 2048
NOCC = 512


def shards(integral_tiles, tile_index, virtual_coeff, occupied_coeff):
    tensor_at = lax.axis_index("tensor")
    row_at = lax.axis_index("row")
    col_at = lax.axis_index("col")
    tensor_count = lax.axis_size("tensor")
    row_count = lax.axis_size("row")
    col_count = lax.axis_size("col")
    held = integral_tiles.shape[0]
    aux_blocks = tensor_count * AB
    mu_blocks = row_count * MB
    quarters = tensor_count * 2
    qsize = TB // quarters
    assert row_count == 2 * PB and quarters * qsize == TB
    tiles = integral_tiles.reshape(held, PB, 2, tensor_count, qsize, TB)
    send = tiles.transpose(3, 1, 2, 0, 4, 5).reshape(tensor_count * row_count, held, qsize * TB)
    recv = lax.all_to_all(send, ("tensor", "row"), split_axis=0, concat_axis=0, tiled=True)
    recv = recv.reshape(tensor_count * row_count * held, qsize * TB)
    index = lax.all_gather(tile_index, ("tensor", "row"), axis=0, tiled=True)
    local_nu = index[:, 2] - col_at * NBC
    block = (index[:, 0] * NBC + local_nu) * mu_blocks + index[:, 1]
    blocks = aux_blocks * NBC * mu_blocks
    selector = (jnp.arange(blocks)[:, None] == block[None, :]).astype(jnp.bfloat16)
    dense = jnp.dot(selector, recv, preferred_element_type=jnp.float32).astype(jnp.bfloat16)
    dense = dense.reshape(aux_blocks, NBC, mu_blocks, qsize, TB)
    occ_all = lax.all_gather(occupied_coeff, "row", axis=0, tiled=True)
    quarter = 2 * (row_at % 2) + tensor_at
    occ_q = lax.dynamic_index_in_dim(
        occ_all.reshape(mu_blocks, quarters, qsize, NOCC), quarter, axis=1, keepdims=False
    )
    partial = jnp.einsum("anmuw,mui->anwi", dense, occ_q, preferred_element_type=jnp.float32)
    pair = lax.psum_scatter(partial.astype(jnp.bfloat16), "tensor", scatter_dimension=0, tiled=True)
    side = row_at % 2
    keep = lax.dynamic_index_in_dim(pair, side, axis=0, keepdims=False)
    give = lax.dynamic_index_in_dim(pair, 1 - side, axis=0, keepdims=False)
    got = lax.ppermute(give, "row", perm=[(i, i ^ 1) for i in range(row_count)])
    occ_done = (keep.astype(jnp.float32) + got.astype(jnp.float32)).astype(jnp.bfloat16)
    chunk = NV // (row_count * col_count)
    virt = virtual_coeff.reshape(NBC, TB, row_count, col_count, chunk)
    z = jnp.einsum("nwi,nwrcj->crji", occ_done, virt, preferred_element_type=jnp.float32)
    z = z.astype(jnp.bfloat16).reshape(col_count * row_count * chunk, NOCC)
    w = lax.psum_scatter(z, "col", scatter_dimension=0, tiled=True).reshape(row_count, chunk, NOCC)
    got_rows = lax.all_to_all(w, "row", split_axis=0, concat_axis=0, tiled=True)
    out = got_rows.reshape(PB, 2, chunk, NOCC).transpose(2, 1, 0, 3)
    return out.reshape(chunk, AB * PB, NOCC)


def solution(mesh):
    in_specs = (
        P(("tensor", "row", "col"), None, None),
        P(("tensor", "row", "col"), None),
        P("col", None),
        P("row", None),
    )
    out_specs = P(("row", "col"), "tensor", None)
    return jax.shard_map(shards, mesh=mesh, in_specs=in_specs, out_specs=out_specs, check_vma=False)
```

profile of v0, /device:TPU:32, one launch (start us, length us, event | category | flops | bytes accessed | tf_op | source)
XLA Modules:
  0.0 265.2 jit_solution(8073186442823905420)
XLA Ops:
  6.5 0.0 all-gather.3.cloned.1.call-start
  6.5 0.7 all-gather.3.cloned.1.call-update
  7.3 6.9 %reshape.57 = bf16[32,8,2,2,16,64]{5,4,3,2,1,0:T(8,128)(2,1)} reshape(bf16[32,8,4096]{2,1,0:T(8,128)(2,1)} %param.4) | data formatting | bytes 4194304 | tf_op jit(solution)/shard_map/reshape | solution.py:29
  14.2 5.3 %copy.42 = bf16[32,8,2,2,16,64]{5,4,0,2,1,3:T(8,128)(2,1)} copy(bf16[32,8,2,2,16,64]{5,4,3,2,1,0:T(8,128)(2,1)} %reshape.57) | data formatting | bytes 4194304 | tf_op jit(solution)/shard_map/reshape | solution.py:29
  19.5 0.0 copy-start.1
  19.5 6.5 %reshape.58 = bf16[32,32,1024]{2,1,0:T(8,128)(2,1)} reshape(bf16[2,8,2,32,16,64]{5,4,3,2,1,0:T(8,128)(2,1)} %bitcast.55) | data formatting | bytes 4194304 | tf_op jit(solution)/shard_map/reshape | solution.py:30
  26.0 7.3 %all-to-all-start = ((bf16[32,32,1024]{2,1,0:T(8,128)(2,1)}), bf16[32,32,1024]{2,1,0:T(8,128)(2,1)S(1)}, u32[]{:S(2)}, u32[]{:S(2)}) async-start(bf16[32,32,1024]{2,1,0:T(8,128)(2,1)} %reshape.58), calls=%async_computation | async-start | bytes 4194304 | tf_op jit(solution)/shard_map/all_to_all | solution.py:31
  33.4 0.0 reduce-scatter.3.cloned.1.call-start
  33.4 0.0 copy-done.1
  33.5 86.8 %all-gather = s32[32,32,3]{1,2,0:T(4,128)S(1)} all-gather(s32[1,32,3]{1,2,0:T(4,128)S(1)} %bitcast.62), channel_id=1, replica_groups=mesh['tensor'=2,'row'=16,'col'=8] {'tensor','row'}, dimensions={0}, use_global_device_ids=true | all-gather | bytes 12672 | tf_op jit(solution)/shard_map/all_gather | solution.py:33
  120.3 0.1 reshape.69
  120.4 0.0 all-to-all-done
  120.4 6.0 %fusion.4 = bf16[2048,1024]{1,0:T(8,128)(2,1)} fusion(bf16[1024,1024]{1,0:T(8,128)(2,1)S(1)} %bitcast.57, s32[1024]{0:T(1024)S(1)} %bitcast.61), kind=kOutput, calls=%fused_computation.8 | convolution fusion | flops 4299161600 | bytes 6295552 | tf_op jit(solution)/shard_map/dot_general | solution.py:38
  126.4 11.6 %reshape.60 = bf16[4,16,32,16,64]{4,3,2,1,0:T(8,128)(2,1)} reshape(bf16[2048,1024]{1,0:T(8,128)(2,1)} %fusion.4) | data formatting | bytes 8388608 | tf_op jit(solution)/shard_map/reshape | solution.py:39
  138.0 0.0 all-gather.3.cloned.1.call-done
  138.0 7.8 %bitcast_convert_fusion = bf16[4,16,64,512]{3,2,1,0:T(8,128)(2,1)} fusion(bf16[4,16,32,16,64]{4,3,2,1,0:T(8,128)(2,1)} %reshape.60, bf16[32,4,16,512]{3,2,1,0:T(8,128)(2,1)} %bitcast.60, s32[]{:T(128)S(6)} %select_n.21), kind=kOutput, calls=%fused_computation | convolution fusion | flops 2149580800 | bytes 13107204 | tf_op jit(solution)/shard_map/anmuw,mui->anwi/dot_general | solution.py:45
  145.8 0.0 reduce-scatter.3.cloned.1.call-update
  145.8 0.0 reduce-scatter.5.cloned.1.call-start
  145.9 17.0 %reduce-scatter.3.cloned.1.call-done = bf16[2,16,64,512]{3,2,1,0:T(8,128)(2,1)} async-done(((bf16[4,16,64,512]{3,2,1,0:T(8,128)(2,1)}), bf16[2,16,64,512]{3,2,1,0:T(8,128)(2,1)}) %reduce-scatter.3.cloned.1.call-update) | async-done | bytes 2097168 | tf_op jit(solution)/shard_map/reduce_scatter | solution.py:46
  162.9 1.3 dynamic-slice_bitcast_fusion
  164.2 1.7 collective-permute-start
  165.9 6.4 %copy.25 = bf16[1024,2048]{0,1:T(8,128)(2,1)} copy(bf16[1024,2048]{1,0:T(8,128)(2,1)} %param.6) | data formatting | bytes 8388608 | tf_op args[2]
  172.3 0.0 copy-start
  172.3 11.8 %reshape.62 = bf16[16,64,16,8,16]{1,0,4,3,2:T(8,128)(2,1)} reshape(bf16[1024,2048]{0,1:T(8,128)(2,1)} %copy.25) | data formatting | bytes 8388608 | tf_op jit(solution)/shard_map/reshape | solution.py:53
  184.1 5.8 %collective-permute-done = bf16[16,64,512]{2,1,0:T(8,128)(2,1)} collective-permute-done((bf16[16,64,512]{2,1,0:T(8,128)(2,1)S(1)}, bf16[16,64,512]{2,1,0:T(8,128)(2,1)}, u32[]{:S(2)}, u32[]{:S(2)}) %collective-permute-start) | collective-permute-done | bytes 1048608 | tf_op jit(solution)/shard_map/ppermute | solution.py:50
  189.8 0.0 copy-done
  189.8 8.0 %fusion.8 = bf16[8,16,16,512]{3,2,0,1:T(8,128)(2,1)S(1)} fusion(bf16[16,64,16,8,16]{1,0,4,3,2:T(8,128)(2,1)} %reshape.62, bf16[16,64,512]{2,1,0:T(8,128)(2,1)} %collective-permute-done, bf16[2,16,64,512]{3,2,1,0:T(8,128)(2,1)S(1)} %copy-done, s32[]{:T(128)S(6)} %select_n.22), kind=kOutput, calls=%fused_computation.11 | convolution fusion | flops 2150629376 | bytes 8388612 | tf_op jit(solution)/shard_map/nwi,nwrcj->crji/dot_general | solution.py:54
  197.8 1.5 copy.27
  199.3 0.0 reduce-scatter.5.cloned.1.call-update
  199.4 42.9 %reduce-scatter.5.cloned.1.call-done = bf16[256,512]{1,0:T(8,128)(2,1)} async-done(((bf16[2048,512]{1,0:T(8,128)(2,1)}), bf16[256,512]{1,0:T(8,128)(2,1)}) %reduce-scatter.5.cloned.1.call-update) | async-done | bytes 262160 | tf_op jit(solution)/shard_map/reduce_scatter | solution.py:56
  242.3 15.5 %all_to_all.10 = bf16[16,16,512]{2,1,0:T(8,128)(2,1)S(1)} all-to-all(bf16[16,16,512]{2,1,0:T(8,128)(2,1)} %bitcast.59), channel_id=1, replica_groups=mesh['tensor'=2,'row'=16,'col'=8] {'row'}, dimensions={0} | all-to-all | bytes 524288 | tf_op jit(solution)/shard_map/all_to_all | solution.py:57
  257.8 0.9 copy.43
  (2 shorter events, 0.0 us)
Async XLA Ops:
  6.5 131.5 %all-gather.3.cloned.1.call-start = ((), (), s32[]{:S(2)}) async-start(), calls=%async_computation.4 | async-start | bytes 2228224 | tf_op jit(solution)/shard_map/all_gather | solution.py:40
  19.5 13.9 %copy-start.1 = (s32[32,3]{0,1:T(4,128)S(1)}, s32[32,3]{0,1:T(4,128)}, u32[]{:S(2)}) copy-start(s32[32,3]{0,1:T(4,128)} %param.5) | copy-start | bytes 1156
  26.0 94.3 %all-to-all-start = ((bf16[32,32,1024]{2,1,0:T(8,128)(2,1)}), bf16[32,32,1024]{2,1,0:T(8,128)(2,1)S(1)}, u32[]{:S(2)}, u32[]{:S(2)}) async-start(bf16[32,32,1024]{2,1,0:T(8,128)(2,1)} %reshape.58), calls=%async_computation | async-start | bytes 4194304 | tf_op jit(solution)/shard_map/all_to_all | solution.py:31
  33.4 129.5 %reduce-scatter.3.cloned.1.call-start = ((), (), s32[]{:S(2)}) async-start(), calls=%async_computation.5 | async-start | bytes 6291456 | tf_op jit(solution)/shard_map/reduce_scatter | solution.py:46
  145.8 96.5 %reduce-scatter.5.cloned.1.call-start = ((), (), s32[]{:S(2)}) async-start(), calls=%async_computation.6 | async-start | bytes 2359296 | tf_op jit(solution)/shard_map/reduce_scatter | solution.py:56
  164.2 25.6 %collective-permute-start = (bf16[16,64,512]{2,1,0:T(8,128)(2,1)S(1)}, bf16[16,64,512]{2,1,0:T(8,128)(2,1)}, u32[]{:S(2)}, u32[]{:S(2)}) collective-permute-start(bf16[16,64,512]{2,1,0:T(8,128)(2,1)S(1)} %dynamic-slice_bitcast_fusion), channel_id=1, source_target_pairs={{0,8},{8,0},{16,24},{24,16},{32,40},{40,32},{48,56},{56,48},{64,72... | collective-permute-start | bytes 3145736 | tf_op jit(solution)/shard_map/ppermute | solution.py:50
  172.3 17.5 %copy-start = (bf16[2,16,64,512]{3,2,1,0:T(8,128)(2,1)S(1)}, bf16[2,16,64,512]{3,2,1,0:T(8,128)(2,1)}, u32[]{:S(2)}) copy-start(bf16[2,16,64,512]{3,2,1,0:T(8,128)(2,1)} %reduce-scatter.3.cloned.1.call-done) | copy-start | bytes 6291460
Sparse Core Ops, SparseCore 0:
  9.8 63.4 all-gather.2
  145.9 16.8 reduce-scatter.2
  199.5 42.7 reduce-scatter.4
where the time goes:
time: 266 us; the launch traced here: 265 us
  blocking collectives  102 us (38%)
  waiting for transfers between devices  66.4 us (25%)
  local copies, waits for them, and re-layouts  52.3 us (20%)
  matrix products  21.8 us (8%)
  between operations  13.2 us (5%)
  starting transfers between devices  9.15 us (3%)
    all_gather x1, blocking collectives, shards(): index = lax.all_gather(tile_index, ('tensor', 'row'), axis=0, tiled=True)  86.8 us
    reduce_scatter x1, waiting for transfers between devices, shards(): lax.psum_scatter(z, 'col', scatter_dimension=0, tiled=True)  42.9 us
    reduce_scatter x1, waiting for transfers between devices, shards(): lax.psum_scatter(partial.astype(jnp.bfloat16), 'tensor', scatter_dimensio...  17 us
    all_to_all x1, blocking collectives, shards(): got_rows = lax.all_to_all(w, 'row', split_axis=0, concat_axis=0, tiled=True)  15.5 us
    reshape x2, local copies, waits for them, and re-layouts, shards(): tiles = integral_tiles.reshape(held, PB, 2, tensor_count, qsize, TB)  12.3 us
    reshape x1, local copies, waits for them, and re-layouts, shards(): virt = virtual_coeff.reshape(NBC, TB, row_count, col_count, chunk)  11.8 us
    reshape x1, local copies, waits for them, and re-layouts, shards(): dense = dense.reshape(aux_blocks, NBC, mu_blocks, qsize, TB)  11.6 us
    dot_general x1, matrix products, shards(): jnp.einsum('nwi,nwrcj->crji', occ_done, virt, preferred_element_type=jnp....  7.97 us
  transfers between devices with their start and end apart: 5, of which 3 were waited for; matrix products, arithmetic and copies ran while one was open for 21% of the time, Pallas kernels for 0%

commit v1 on v0

--- a/solution.py
+++ b/solution.py
@@ -11,6 +11,14 @@
 CAP = 2
 NV = 2048
 NOCC = 512
+
+
+def tiled_gather(shard, axis, dim):
+    size = lax.axis_size(axis)
+    repeats = [size if d == dim else 1 for d in range(shard.ndim)]
+    return lax.all_to_all(
+        jnp.tile(shard, repeats), axis, split_axis=dim, concat_axis=dim, tiled=True
+    )
 
 
 def shards(integral_tiles, tile_index, virtual_coeff, occupied_coeff):
@@ -30,7 +38,7 @@
     send = tiles.transpose(3, 1, 2, 0, 4, 5).reshape(tensor_count * row_count, held, qsize * TB)
     recv = lax.all_to_all(send, ("tensor", "row"), split_axis=0, concat_axis=0, tiled=True)
     recv = recv.reshape(tensor_count * row_count * held, qsize * TB)
-    index = lax.all_gather(tile_index, ("tensor", "row"), axis=0, tiled=True)
+    index = tiled_gather(tile_index, ("tensor", "row"), 0)
     local_nu = index[:, 2] - col_at * NBC
     block = (index[:, 0] * NBC + local_nu) * mu_blocks + index[:, 1]
     blocks = aux_blocks * NBC * mu_blocks

time: 266 us -> 225 us (0.85)
  blocking collectives: 102 us -> 15.2 us
  waiting for transfers between devices: 66.4 us -> 104 us
  starting transfers between devices: 9.15 us -> 16.5 us
    all_gather x1 -> x0, blocking collectives: 86.8 us -> none  [shards(): index = lax.all_gather(tile_index, ('tensor', 'row'), axis=0, tiled=True)]
    all_to_all x1, waiting for transfers between devices: 0.01 us -> 35.3 us  [shards(): lax.all_to_all(send, ('tensor', 'row'), split_axis=0, concat_axis=0, tile...]
    all_to_all x0 -> x1, starting transfers between devices: none -> 7.32 us  [tiled_gather(): lax.all_to_all(jnp.tile(shard, repeats), axis, split_axis=dim, concat_axi...]
    unnamed x6 -> x3, local copies, waits for them, and re-layouts: 6.47 us -> 6.4 us
  transfers between devices with their start and end apart: 5 -> 6, of which waited for: 3 -> 4; matrix products, arithmetic and copies ran while one was open for 21% -> 25% of each run, Pallas kernels for 0% -> 0%
where the time goes in v1:
time: 225 us; the launch traced here: 224 us
  waiting for transfers between devices  104 us (46%)
  local copies, waits for them, and re-layouts  53.7 us (24%)
  matrix products  21.8 us (10%)
  starting transfers between devices  16.5 us (7%)
  blocking collectives  15.2 us (7%)
  between operations  13.2 us (6%)
    reduce_scatter x1, waiting for transfers between devices, shards(): lax.psum_scatter(z, 'col', scatter_dimension=0, tiled=True)  43.2 us
    all_to_all x1, waiting for transfers between devices, shards(): lax.all_to_all(send, ('tensor', 'row'), split_axis=0, concat_axis=0, tile...  35.3 us
    reduce_scatter x1, waiting for transfers between devices, shards(): lax.psum_scatter(partial.astype(jnp.bfloat16), 'tensor', scatter_dimensio...  18.6 us
    all_to_all x1, blocking collectives, shards(): got_rows = lax.all_to_all(w, 'row', split_axis=0, concat_axis=0, tiled=True)  15.2 us
    reshape x2, local copies, waits for them, and re-layouts, shards(): tiles = integral_tiles.reshape(held, PB, 2, tensor_count, qsize, TB)  12.3 us
    reshape x1, local copies, waits for them, and re-layouts, shards(): virt = virtual_coeff.reshape(NBC, TB, row_count, col_count, chunk)  11.7 us
    reshape x1, local copies, waits for them, and re-layouts, shards(): dense = dense.reshape(aux_blocks, NBC, mu_blocks, qsize, TB)  11.6 us
    dot_general x1, matrix products, shards(): jnp.einsum('nwi,nwrcj->crji', occ_done, virt, preferred_element_type=jnp....  7.97 us
  transfers between devices with their start and end apart: 6, of which 4 were waited for; matrix products, arithmetic and copies ran while one was open for 25% of the time, Pallas kernels for 0%

profile of v1, /device:TPU:32, one launch (start us, length us, event | category | flops | bytes accessed | tf_op | source)
XLA Modules:
  0.0 223.9 jit_solution(2024560122701207661)
XLA Ops:
  6.5 0.0 all-gather.2.cloned.1.call-start
  6.5 0.7 all-gather.2.cloned.1.call-update
  7.3 1.3 tile.2
  8.6 7.3 %all-to-all-start = ((s32[32,32,3]{1,2,0:T(4,128)}), s32[32,32,3]{1,2,0:T(4,128)S(1)}, u32[]{:S(2)}, u32[]{:S(2)}) async-start(s32[32,32,3]{1,2,0:T(4,128)} %tile.2), calls=%async_computation | async-start | bytes 131072 | tf_op jit(solution)/shard_map/all_to_all | solution.py:19
  15.9 6.9 %reshape.64 = bf16[32,8,2,2,16,64]{5,4,3,2,1,0:T(8,128)(2,1)} reshape(bf16[32,8,4096]{2,1,0:T(8,128)(2,1)} %param.4) | data formatting | bytes 4194304 | tf_op jit(solution)/shard_map/reshape | solution.py:37
  22.8 5.4 %copy.47 = bf16[32,8,2,2,16,64]{5,4,0,2,1,3:T(8,128)(2,1)} copy(bf16[32,8,2,2,16,64]{5,4,3,2,1,0:T(8,128)(2,1)} %reshape.64) | data formatting | bytes 4194304 | tf_op jit(solution)/shard_map/reshape | solution.py:37
  28.2 6.5 %reshape.65 = bf16[32,32,1024]{2,1,0:T(8,128)(2,1)} reshape(bf16[2,8,2,32,16,64]{5,4,3,2,1,0:T(8,128)(2,1)} %bitcast.54) | data formatting | bytes 4194304 | tf_op jit(solution)/shard_map/reshape | solution.py:38
  34.7 0.0 all-to-all-done
  34.7 7.4 %all-to-all-start.1 = ((bf16[32,32,1024]{2,1,0:T(8,128)(2,1)}), bf16[32,32,1024]{2,1,0:T(8,128)(2,1)S(1)}, u32[]{:S(2)}, u32[]{:S(2)}) async-start(bf16[32,32,1024]{2,1,0:T(8,128)(2,1)} %reshape.65), calls=%async_computation.1 | async-start | bytes 4194304 | tf_op jit(solution)/shard_map/all_to_all | solution.py:39
  42.1 0.0 reduce-scatter.3.cloned.1.call-start
  42.2 0.1 all_to_all.13
  42.3 35.3 %all-to-all-done.1 = bf16[32,32,1024]{2,1,0:T(8,128)(2,1)S(1)} async-done(((bf16[32,32,1024]{2,1,0:T(8,128)(2,1)}), bf16[32,32,1024]{2,1,0:T(8,128)(2,1)S(1)}, u32[]{:S(2)}, u32[]{:S(2)}) %all-to-all-start.1) | async-done | bytes 2097184 | tf_op jit(solution)/shard_map/all_to_all | solution.py:39
  77.7 6.0 %fusion.4 = bf16[2048,1024]{1,0:T(8,128)(2,1)} fusion(bf16[1024,1024]{1,0:T(8,128)(2,1)S(1)} %bitcast.56, s32[1024]{0:T(1024)S(1)} %bitcast.60), kind=kOutput, calls=%fused_computation.8 | convolution fusion | flops 4299161600 | bytes 6295552 | tf_op jit(solution)/shard_map/dot_general | solution.py:46
  83.7 11.6 %reshape.67 = bf16[4,16,32,16,64]{4,3,2,1,0:T(8,128)(2,1)} reshape(bf16[2048,1024]{1,0:T(8,128)(2,1)} %fusion.4) | data formatting | bytes 8388608 | tf_op jit(solution)/shard_map/reshape | solution.py:47
  95.3 0.0 all-gather.2.cloned.1.call-done
  95.3 7.8 %bitcast_convert_fusion = bf16[4,16,64,512]{3,2,1,0:T(8,128)(2,1)} fusion(bf16[4,16,32,16,64]{4,3,2,1,0:T(8,128)(2,1)} %reshape.67, bf16[32,4,16,512]{3,2,1,0:T(8,128)(2,1)} %bitcast.59, s32[]{:T(128)S(6)} %select_n.21), kind=kOutput, calls=%fused_computation | convolution fusion | flops 2149580800 | bytes 13107204 | tf_op jit(solution)/shard_map/anmuw,mui->anwi/dot_general | solution.py:53
  103.1 0.0 reduce-scatter.3.cloned.1.call-update
  103.1 0.0 reduce-scatter.5.cloned.1.call-start
  103.1 18.6 %reduce-scatter.3.cloned.1.call-done = bf16[2,16,64,512]{3,2,1,0:T(8,128)(2,1)} async-done(((bf16[4,16,64,512]{3,2,1,0:T(8,128)(2,1)}), bf16[2,16,64,512]{3,2,1,0:T(8,128)(2,1)}) %reduce-scatter.3.cloned.1.call-update) | async-done | bytes 2097168 | tf_op jit(solution)/shard_map/reduce_scatter | solution.py:54
  121.7 1.3 dynamic-slice_bitcast_fusion
  123.0 1.7 collective-permute-start
  124.8 6.4 %copy.30 = bf16[1024,2048]{0,1:T(8,128)(2,1)} copy(bf16[1024,2048]{1,0:T(8,128)(2,1)} %param.6) | data formatting | bytes 8388608 | tf_op args[2]
  131.2 0.0 copy-start
  131.2 11.7 %reshape.69 = bf16[16,64,16,8,16]{1,0,4,3,2:T(8,128)(2,1)} reshape(bf16[1024,2048]{0,1:T(8,128)(2,1)} %copy.30) | data formatting | bytes 8388608 | tf_op jit(solution)/shard_map/reshape | solution.py:61
  142.9 5.7 %collective-permute-done = bf16[16,64,512]{2,1,0:T(8,128)(2,1)} collective-permute-done((bf16[16,64,512]{2,1,0:T(8,128)(2,1)S(1)}, bf16[16,64,512]{2,1,0:T(8,128)(2,1)}, u32[]{:S(2)}, u32[]{:S(2)}) %collective-permute-start) | collective-permute-done | bytes 1048608 | tf_op jit(solution)/shard_map/ppermute | solution.py:58
  148.7 0.0 copy-done
  148.7 8.0 %fusion.8 = bf16[8,16,16,512]{3,2,0,1:T(8,128)(2,1)S(1)} fusion(bf16[16,64,16,8,16]{1,0,4,3,2:T(8,128)(2,1)} %reshape.69, bf16[16,64,512]{2,1,0:T(8,128)(2,1)} %collective-permute-done, bf16[2,16,64,512]{3,2,1,0:T(8,128)(2,1)S(1)} %copy-done, s32[]{:T(128)S(6)} %select_n.22), kind=kOutput, calls=%fused_computation.11 | convolution fusion | flops 2150629376 | bytes 8388612 | tf_op jit(solution)/shard_map/nwi,nwrcj->crji/dot_general | solution.py:62
  156.6 1.5 copy.32
  158.2 0.0 reduce-scatter.5.cloned.1.call-update
  158.2 43.2 %reduce-scatter.5.cloned.1.call-done = bf16[256,512]{1,0:T(8,128)(2,1)} async-done(((bf16[2048,512]{1,0:T(8,128)(2,1)}), bf16[256,512]{1,0:T(8,128)(2,1)}) %reduce-scatter.5.cloned.1.call-update) | async-done | bytes 262160 | tf_op jit(solution)/shard_map/reduce_scatter | solution.py:64
  201.4 15.2 %all_to_all.19 = bf16[16,16,512]{2,1,0:T(8,128)(2,1)S(1)} all-to-all(bf16[16,16,512]{2,1,0:T(8,128)(2,1)} %bitcast.58), channel_id=1, replica_groups=mesh['tensor'=2,'row'=16,'col'=8] {'row'}, dimensions={0} | all-to-all | bytes 524288 | tf_op jit(solution)/shard_map/all_to_all | solution.py:65
  216.5 0.9 copy.48
  (2 shorter events, 0.0 us)
Async XLA Ops:
  6.5 88.7 %all-gather.2.cloned.1.call-start = ((), (), s32[]{:S(2)}) async-start(), calls=%async_computation.5 | async-start | bytes 2228224 | tf_op jit(solution)/shard_map/all_gather | solution.py:48
  8.6 26.1 %all-to-all-start = ((s32[32,32,3]{1,2,0:T(4,128)}), s32[32,32,3]{1,2,0:T(4,128)S(1)}, u32[]{:S(2)}, u32[]{:S(2)}) async-start(s32[32,32,3]{1,2,0:T(4,128)} %tile.2), calls=%async_computation | async-start | bytes 131072 | tf_op jit(solution)/shard_map/all_to_all | solution.py:19
  34.7 42.9 %all-to-all-start.1 = ((bf16[32,32,1024]{2,1,0:T(8,128)(2,1)}), bf16[32,32,1024]{2,1,0:T(8,128)(2,1)S(1)}, u32[]{:S(2)}, u32[]{:S(2)}) async-start(bf16[32,32,1024]{2,1,0:T(8,128)(2,1)} %reshape.65), calls=%async_computation.1 | async-start | bytes 4194304 | tf_op jit(solution)/shard_map/all_to_all | solution.py:39
  42.1 79.6 %reduce-scatter.3.cloned.1.call-start = ((), (), s32[]{:S(2)}) async-start(), calls=%async_computation.6 | async-start | bytes 6291456 | tf_op jit(solution)/shard_map/reduce_scatter | solution.py:54
  103.1 98.3 %reduce-scatter.5.cloned.1.call-start = ((), (), s32[]{:S(2)}) async-start(), calls=%async_computation.7 | async-start | bytes 2359296 | tf_op jit(solution)/shard_map/reduce_scatter | solution.py:64
  123.0 25.6 %collective-permute-start = (bf16[16,64,512]{2,1,0:T(8,128)(2,1)S(1)}, bf16[16,64,512]{2,1,0:T(8,128)(2,1)}, u32[]{:S(2)}, u32[]{:S(2)}) collective-permute-start(bf16[16,64,512]{2,1,0:T(8,128)(2,1)S(1)} %dynamic-slice_bitcast_fusion), channel_id=1, source_target_pairs={{0,8},{8,0},{16,24},{24,16},{32,40},{40,32},{48,56},{56,48},{64,72... | collective-permute-start | bytes 3145736 | tf_op jit(solution)/shard_map/ppermute | solution.py:58
  131.2 17.5 %copy-start = (bf16[2,16,64,512]{3,2,1,0:T(8,128)(2,1)S(1)}, bf16[2,16,64,512]{3,2,1,0:T(8,128)(2,1)}, u32[]{:S(2)}) copy-start(bf16[2,16,64,512]{3,2,1,0:T(8,128)(2,1)} %reduce-scatter.3.cloned.1.call-done) | copy-start | bytes 6291460
Sparse Core Ops, SparseCore 0:
  9.8 68.8 all-gather.1
  103.2 18.4 reduce-scatter.2
  158.3 43.0 reduce-scatter.4
